TPU v7x, 256 devices: a whole 4x4x8 slice. The times are simulated.
256 devices in a mesh: grp: 32 (over z, x), tp: 8 (over y, core).
Axes of the slice: x: 4, y: 4, z: 8, core: 2. Of those that a mesh axis runs over, the one named last changes fastest.
Arguments:
- tokens: bfloat16 [32768, 2048], P('grp'), may hold values from -6 to 6
- norm_gain: float32 [2048], replicated, may hold values from 0.5 to 7
- w_qkv: bfloat16 [2048, 3, 2048], P(None, None, 'tp'), may hold values from -0.125 to 0.125
- w_out: bfloat16 [2048, 2048], P('tp'), may hold values from -0.125 to 0.125
- a_in: bfloat16 [64, 2048, 48], P('grp', 'tp'), may hold values from -0.125 to 0.125
- b_in: bfloat16 [64, 3, 16, 2048], P('grp', None, None, 'tp'), may hold values from -1.5 to 1.5
- a_out: bfloat16 [64, 2048, 16], P('grp', 'tp'), may hold values from -0.125 to 0.125
- b_out: bfloat16 [64, 16, 2048], P('grp', None, 'tp'), may hold values from -1.5 to 1.5
- req_len: int32 [32, 4], replicated, may hold values from 1 to 512, 1024 in all within a row
- req_adapter: int32 [32, 4], replicated, may hold values from 0 to 63, as said below
- holder: int32 [64], replicated, may hold values from 0 to 63, each once
- page_table: int32 [32, 8], P('grp'), may hold values from 0 to 7, each once within a row
Outputs:
- layer_out: bfloat16 [32768, 2048], P('grp', 'tp')
- kv_pages: bfloat16 [256, 2, 128, 2048], P('grp', None, None, 'tp')
Inputs may be any that keep to these rules, and one draw needn't show every extreme that they name: `req_adapter`: exactly 16 different adapters appear among all requests.
All inputs are finite; a program needn't handle non-finite values.
Results may differ from a plain program's by a relative error of at most 0.017.
The roundings to bfloat16 on the way count: a program that leaves them out, or rounds other values in their place, can miss the bound.
Values may be sent and summed in bfloat16 or wider, within the bound.
No kernel may reach another device: no remote copies, remote signals or barrier semaphores. Data moves between devices by JAX's collectives and lax.ppermute only.
A program may use at most 128 MiB of HBM per device.

v0:
```python
import math
import jax
import jax.numpy as jnp
from jax import lax
from jax.sharding import PartitionSpec as P

HD = 128
PAGE = 128
EPSILON = 1e-05
THETA = 10000.0


def shifted(block, axis, distance):
    devices = range(lax.axis_size(axis))
    route = [(i - distance, i) for i in devices if i - distance in devices]
    return lax.ppermute(block, axis, route)


USED = 16


def xor_allreduce(value, axis):
    count = lax.axis_size(axis)
    step = 1
    while step < count:
        route = [(i, i ^ step) for i in range(count)]
        value = value + lax.ppermute(value, axis, route)
        step *= 2
    return value


def fetch_adapters(stores, req_adapter, holder, wanted, group_id):
    held = stores[0].shape[0]
    total = holder.shape[0]
    names = jnp.arange(total, dtype=jnp.int32)
    used = jnp.any(req_adapter.reshape(-1)[:, None] == names[None, :], axis=0)
    rank = jnp.cumsum(used.astype(jnp.int32)) - 1
    picks = jnp.arange(USED, dtype=jnp.int32)
    hit = used[None, :] & (rank[None, :] == picks[:, None])
    chosen = jnp.sum(jnp.where(hit, names[None, :], 0), axis=1)
    slots = holder[chosen]
    mine = slots // held == group_id
    local_idx = slots % held
    flat = jnp.concatenate([s.reshape(held, -1) for s in stores], axis=1)
    compact = jnp.where(mine[:, None], jnp.take(flat, local_idx, axis=0), jnp.zeros((), flat.dtype))
    compact = lax.psum(compact, "grp")
    mine_rows = jnp.take(compact, rank[wanted], axis=0)
    out = []
    at = 0
    for s in stores:
        size = math.prod(s.shape[1:])
        out.append(mine_rows[:, at : at + size].reshape((wanted.shape[0],) + s.shape[1:]))
        at += size
    return tuple(out)


def rms_norm(token_rows, norm_gain):
    values = token_rows.astype(jnp.float32)
    norm_scale = lax.rsqrt(jnp.mean(values * values, axis=-1, keepdims=True) + EPSILON)
    return (values * norm_scale * norm_gain).astype(jnp.bfloat16)


def request_layout(lengths, offset, tok_count):
    end_at = jnp.cumsum(lengths)
    starts = end_at - lengths
    row_ids = jnp.arange(tok_count, dtype=jnp.int32)
    segment = jnp.sum((row_ids[:, None] >= end_at[None, :]).astype(jnp.int32), axis=1)
    member = segment[:, None] == jnp.arange(lengths.shape[0], dtype=jnp.int32)[None, :]
    begin_at = jnp.sum(jnp.where(member, starts[None, :], 0), axis=1)
    position = row_ids - begin_at + jnp.where(segment == 0, offset, 0)
    return (segment, member, position)


def rotate(head_rows, position, head_dim):
    half_dim = head_dim // 2
    frequency = THETA ** (-(jnp.arange(half_dim, dtype=jnp.float32) * (2.0 / head_dim)))
    angles = position.astype(jnp.float32)[:, None] * frequency[None, :]
    cosine = jnp.cos(angles)[:, None, :]
    sine_part = jnp.sin(angles)[:, None, :]
    lower_half = head_rows[..., :half_dim]
    upper_half = head_rows[..., half_dim:]
    return jnp.concatenate(
        [
            lower_half * cosine - upper_half * sine_part,
            upper_half * cosine + lower_half * sine_part,
        ],
        axis=-1,
    )


def local(
    tokens,
    norm_gain,
    w_qkv,
    w_out,
    a_in,
    b_in,
    a_out,
    b_out,
    req_len,
    req_adapter,
    holder,
    page_table,
):
    tok_count = tokens.shape[0]
    local_width = w_out.shape[0]
    local_heads = local_width // HD
    req_count = req_len.shape[1]
    rank_dim = a_out.shape[2]
    group_id = lax.axis_index("grp")
    tp_id = lax.axis_index("tp")
    lengths = lax.dynamic_index_in_dim(req_len, group_id, 0, keepdims=False)
    earlier = lax.dynamic_index_in_dim(req_len, jnp.maximum(group_id - 1, 0), 0, keepdims=False)
    continued = group_id > 0
    prev_len = earlier[req_count - 1]
    offset = jnp.where(continued, prev_len, 0)
    segment, member, position = request_layout(lengths, offset, tok_count)
    wanted = lax.dynamic_index_in_dim(req_adapter, group_id, 0, keepdims=False)
    sel_in, sel_up, sel_odown, sel_oup = fetch_adapters(
        (a_in, b_in, a_out, b_out), req_adapter, holder, wanted, group_id
    )
    member_f = member.astype(jnp.float32)
    pick_bf = member.astype(jnp.bfloat16)
    normed = rms_norm(tokens, norm_gain)
    own_cols = lax.dynamic_slice_in_dim(normed, tp_id * local_width, local_width, 1)
    down_f = jnp.einsum("td,rdk->trk", own_cols, sel_in, preferred_element_type=jnp.float32)
    lowrank_f = xor_allreduce(jnp.sum(down_f * member_f[:, :, None], axis=1), "tp")
    lowrank = lowrank_f.astype(jnp.bfloat16)
    spread = (pick_bf[:, :, None] * lowrank[:, None, :]).reshape(tok_count, req_count, 3, rank_dim)
    delta_qkv = jnp.einsum("trck,rckd->tcd", spread, sel_up, preferred_element_type=jnp.float32)
    base_qkv = jnp.dot(
        normed, w_qkv.reshape(w_qkv.shape[0], 3 * local_width), preferred_element_type=jnp.float32
    )
    qkv = (base_qkv.reshape(tok_count, 3, local_width) + delta_qkv).reshape(
        tok_count, 3, local_heads, HD
    )
    query_rows = rotate(qkv[:, 0], position, HD).astype(jnp.bfloat16)
    key_rows = rotate(qkv[:, 1], position, HD).astype(jnp.bfloat16).reshape(tok_count, local_width)
    value_rows = qkv[:, 2].astype(jnp.bfloat16).reshape(tok_count, local_width)
    row_ids = jnp.arange(tok_count, dtype=jnp.int32)
    far_key, far_value = shifted((key_rows, value_rows), "grp", 1)
    far_ok = continued & (segment[:, None] == 0) & (row_ids[None, :] >= tok_count - prev_len)
    far_count = far_key.shape[0]
    near_ok = (segment[:, None] == segment[None, :]) & (row_ids[None, :] <= row_ids[:, None])
    allowed = jnp.concatenate([far_ok, near_ok], axis=1)
    key_all = jnp.concatenate([far_key, key_rows], axis=0).reshape(
        far_count + tok_count, local_heads, HD
    )
    value_all = jnp.concatenate([far_value, value_rows], axis=0).reshape(
        far_count + tok_count, local_heads, HD
    )
    score_scale = 1.0 / math.sqrt(HD)
    scores = (
        jnp.einsum("thd,shd->hts", query_rows, key_all, preferred_element_type=jnp.float32)
        * score_scale
    )
    scores = jnp.where(allowed[None], scores, -jnp.inf)
    row_top = jnp.max(scores, axis=-1, keepdims=True)
    weights = jnp.exp(scores - row_top)
    weights_bf = (weights / jnp.sum(weights, axis=-1, keepdims=True)).astype(jnp.bfloat16)
    mixed_heads = jnp.einsum(
        "hts,shd->thd", weights_bf, value_all, preferred_element_type=jnp.float32
    )
    attended = mixed_heads.astype(jnp.bfloat16).reshape(tok_count, local_width)
    partial_value = jnp.dot(attended, w_out, preferred_element_type=jnp.float32)
    down_o = jnp.einsum("td,rdk->trk", attended, sel_odown, preferred_element_type=jnp.float32)
    low_part = jnp.sum(down_o * member_f[:, :, None], axis=1).astype(jnp.bfloat16)
    n_tp = lax.axis_size("tp")
    packed = jnp.concatenate(
        [
            partial_value.astype(jnp.bfloat16).reshape(tok_count, n_tp, local_width),
            jnp.broadcast_to(low_part[:, None, :], (tok_count, n_tp, rank_dim)),
        ],
        axis=2,
    ).reshape(tok_count, n_tp * (local_width + rank_dim))
    summed = lax.psum_scatter(packed, "tp", scatter_dimension=1, tiled=True)
    base_out = summed[:, :local_width].astype(jnp.float32)
    low_o = summed[:, local_width:]
    spread_o = (pick_bf[:, :, None] * low_o[:, None, :]).reshape(tok_count, req_count * rank_dim)
    delta_o = jnp.dot(
        spread_o,
        sel_oup.reshape(req_count * rank_dim, local_width),
        preferred_element_type=jnp.float32,
    )
    own_rows = lax.dynamic_slice_in_dim(tokens, tp_id * local_width, local_width, 1).astype(
        jnp.float32
    )
    layer_out = (own_rows + base_out + delta_o).astype(jnp.bfloat16)
    page_row = page_table[0]
    page_count = page_row.shape[0]
    numbers = jnp.arange(page_count, dtype=jnp.int32)
    inverse = jnp.sum(jnp.where(page_row[:, None] == numbers[None, :], numbers[:, None], 0), axis=0)
    both_blocks = jnp.stack(
        [
            key_rows.reshape(page_count, PAGE, local_width),
            value_rows.reshape(page_count, PAGE, local_width),
        ],
        axis=1,
    )
    kv_pages = jnp.take(both_blocks, inverse, axis=0)
    return (layer_out, kv_pages)


def solution(mesh):
    return jax.shard_map(
        local,
        mesh=mesh,
        in_specs=(
            P("grp", None),
            P(),
            P(None, None, "tp"),
            P("tp", None),
            P("grp", "tp", None),
            P("grp", None, None, "tp"),
            P("grp", "tp", None),
            P("grp", None, "tp"),
            P(),
            P(),
            P(),
            P("grp", None),
        ),
        out_specs=(P("grp", "tp"), P("grp", None, None, "tp")),
        check_vma=False,
    )
```

profile of v0, /device:TPU:4, one launch (start us, length us, event | category | flops | bytes accessed | tf_op | source)
XLA Modules:
  0.0 312.4 jit_solution(5977130857267515130)
XLA Ops:
  7.2 0.8 copy.93
  8.0 0.8 copy.63
  9.5 1.3 gather_fusion.1
  10.9 0.8 copy.92
  11.7 0.9 copy.65
  12.8 0.8 copy.66
  14.0 1.2 gather_fusion.2
  15.3 1.2 select_select_fusion
  19.6 3.1 fusion.2
  23.4 4.7 %copy.62 = bf16[2048,3,256]{0,2,1:T(8,128)(2,1)} copy(bf16[2048,3,256]{2,0,1:T(8,128)(2,1)} %param.14) | data formatting | bytes 6291456 | tf_op args[2]
  28.6 3.5 %fusion.4 = bf16[1024,2048]{1,0:T(8,128)(2,1)S(1)} fusion(bf16[1024,2048]{1,0:T(8,128)(2,1)} %param.12, f32[2048]{0:T(1024)S(1)} %copy-done.7, f32[1024]{0:T(1024)S(1)} %add_rsqrt_fusion), kind=kLoop, calls=%fused_computation.14 | loop fusion | flops 8388608 | bytes 8400896 | tf_op jit(solution)/shard_map/convert_element_type | solution.py:60
  32.2 1.9 copy-done.2
  34.1 5.1 %fusion.9 = f32[1024,3,256]{0,2,1:T(8,128)} fusion(bf16[1024,2048]{1,0:T(8,128)(2,1)S(1)} %fusion.4, bf16[2048,3,256]{0,2,1:T(8,128)(2,1)S(1)} %copy-done.3), kind=kOutput, calls=%fused_computation.21 | convolution fusion | flops 3221225472 | bytes 10485760 | tf_op jit(solution)/shard_map/dot_general | solution.py:131
  39.2 129.0 %all-reduce.2.cloned.1.call-done = bf16[16,32768]{1,0:T(8,128)(2,1)} async-done(((bf16[16,32768]{1,0:T(8,128)(2,1)}), bf16[16,32768]{1,0:T(8,128)(2,1)}) %all-reduce.2.cloned.1.call-update) | async-done | bytes 1048592 | tf_op jit(solution)/shard_map/psum | solution.py:46
  168.2 2.4 gather_fusion.3
  172.6 1.4 fusion.21
  174.2 1.5 pad_add_fusion
  175.7 1.6 collective-permute-start.1
  177.3 3.0 multiply_cosine_fusion
  180.3 2.8 collective-permute-done.1
  183.1 3.3 %collective-permute-start.2 = (f32[1024,48]{0,1:T(8,128)S(1)}, f32[1024,48]{0,1:T(8,128)S(1)}, u32[]{:S(2)}, u32[]{:S(2)}) collective-permute-start(f32[1024,48]{0,1:T(8,128)S(1)} %add.163), channel_id=1, source_target_pairs={{0,4},{1,5},{2,6},{3,7},{4,0},{5,1},{6,2},{7,3},{8,12},{9,13},{10,... | collective-permute-start | bytes 589832 | tf_op jit(solution)/shard_map/ppermute | solution.py:27
  186.4 0.8 fusion.47
  187.6 3.7 %collective-permute-done.2 = f32[1024,48]{0,1:T(8,128)S(1)} collective-permute-done((f32[1024,48]{0,1:T(8,128)S(1)}, f32[1024,48]{0,1:T(8,128)S(1)}, u32[]{:S(2)}, u32[]{:S(2)}) %collective-permute-start.2) | collective-permute-done | bytes 196640 | tf_op jit(solution)/shard_map/ppermute | solution.py:27
  191.3 2.5 bitcast_add_fusion
  193.8 0.9 slice.89
  194.8 0.9 copy-done.1
  195.6 1.2 fusion.46
  197.1 3.2 %collective-permute-start.3 = (bf16[1024,256]{0,1:T(8,128)(2,1)}, bf16[1024,256]{0,1:T(8,128)(2,1)}, u32[]{:S(2)}, u32[]{:S(2)}) collective-permute-start(bf16[1024,256]{0,1:T(8,128)(2,1)} %bitcast.106), channel_id=1, source_target_pairs={{0,8},{8,16},{16,24},{24,32},{32,40},{40,48},{48,56},{56,64},{64,7... | collective-permute-start | bytes 1572872 | tf_op jit(solution)/shard_map/ppermute | solution.py:16
  200.3 1.6 copy.89
  201.9 1.6 multiply_subtract_fusion
  203.8 1.0 copy.71
  204.8 4.1 %collective-permute-start.4 = (bf16[1024,256]{0,1:T(8,128)(2,1)}, bf16[1024,256]{0,1:T(8,128)(2,1)}, u32[]{:S(2)}, u32[]{:S(2)}) collective-permute-start(bf16[1024,256]{0,1:T(8,128)(2,1)} %bitcast.29), channel_id=1, source_target_pairs={{0,8},{8,16},{16,24},{24,32},{32,40},{40,48},{48,56},{56,64},{64,7... | collective-permute-start | bytes 1572872 | tf_op jit(solution)/shard_map/ppermute | solution.py:16
  209.0 1.3 slice_bitcast_fusion
  210.3 2.6 subtract_convert_fusion
  212.9 10.3 %collective-permute-done.4 = bf16[1024,256]{0,1:T(8,128)(2,1)} collective-permute-done((bf16[1024,256]{0,1:T(8,128)(2,1)}, bf16[1024,256]{0,1:T(8,128)(2,1)}, u32[]{:S(2)}, u32[]{:S(2)}) %collective-permute-start.4) | collective-permute-done | bytes 524320 | tf_op jit(solution)/shard_map/ppermute | solution.py:16
  223.2 1.3 copy.72
  224.5 10.8 %fusion.49 = (f32[2,1024]{1,0:T(2,128)S(1)}, f32[2,1024,2048]{2,1,0:T(8,128)}) fusion(pred[1024,2048]{1,0:T(8,128)(4,1)} %pad_add_fusion, bf16[1024,2,128]{2,0,1:T(8,128)(2,1)S(1)} %maximum_convert_fusion, bf16[1024,2,128]{2,0,1:T(8,128)(2,1)S(1)} %copy.72, bf16[1024,2,64]{2,0,1:T(8,128)(2,1)} %get-tuple-element.7, bf16[1024,2,64]{2,0,1:T(8,128)(2,1)} %get-tuple-element.6), kind=kOutput, calls=%fused_computation.127 | convolution fusion | flops 1093666816 | bytes 20455424 | tf_op jit(solution)/shard_map/sub | solution.py:159
  235.3 8.9 %fusion.16 = bf16[2,128,1024]{2,1,0:T(8,128)(2,1)S(1)} fusion(f32[2,1024,2048]{2,1,0:T(8,128)} %get-tuple-element.23, f32[2,1024]{1,0:T(2,128)S(1)} %get-tuple-element.22, bf16[1024,2,128]{0,2,1:T(8,128)(2,1)S(1)} %slice_bitcast_fusion, bf16[1024,2,128]{0,2,1:T(8,128)(2,1)} %bitcast.22), kind=kOutput, calls=%fused_computation.32 | convolution fusion | flops 1084489728 | bytes 18358272 | tf_op jit(solution)/shard_map/hts,shd->thd/dot_general | solution.py:161
  244.5 3.2 %convolution_convert_fusion = bf16[1024,2048]{1,0:T(8,128)(2,1)} fusion(bf16[1024,256]{0,1:T(8,128)(2,1)S(1)} %bitcast.104, bf16[256,2048]{1,0:T(8,128)(2,1)S(1)} %copy-done), kind=kOutput, calls=%fused_computation.25 | convolution fusion | flops 1075838976 | bytes 5767168 | tf_op jit(solution)/shard_map/dot_general | solution.py:165
  247.7 6.4 %copy.82 = bf16[1024,2048]{0,1:T(8,128)(2,1)} copy(bf16[1024,2048]{1,0:T(8,128)(2,1)} %convolution_convert_fusion) | data formatting | bytes 8388608 | tf_op jit(solution)/shard_map/reshape | solution.py:171
  254.1 4.7 %pad_maximum_fusion = bf16[1024,8,272]{0,2,1:T(8,128)(2,1)} fusion(bf16[1024,8,16]{0,2,1:T(8,128)(2,1)S(1)} %broadcast_in_dim.158, bf16[1024,8,256]{0,2,1:T(8,128)(2,1)} %bitcast.97), kind=kLoop, calls=%fused_computation.20 | loop fusion | flops 8912896 | bytes 8912896 | tf_op jit(solution)/shard_map/concatenate | solution.py:169
  260.6 1.1 reshape.475
  261.8 1.1 pad_maximum_fusion.2
  263.5 1.1 broadcast_select_fusion
  264.7 36.7 %reduce-scatter.4.cloned.1.call-done = bf16[272,1024]{1,0:T(8,128)(2,1)} async-done(((bf16[2176,1024]{1,0:T(8,128)(2,1)}), bf16[272,1024]{1,0:T(8,128)(2,1)}) %reduce-scatter.4.cloned.1.call-update) | async-done | bytes 557072
  301.3 0.8 slice.78
  302.1 1.1 slice.77
  303.4 2.2 fusion.15
  (90 shorter events, 10.2 us)
Async XLA Ops:
  7.2 237.3 %copy-start = (bf16[256,2048]{1,0:T(8,128)(2,1)S(1)}, bf16[256,2048]{1,0:T(8,128)(2,1)}, u32[]{:S(2)}) copy-start(bf16[256,2048]{1,0:T(8,128)(2,1)} %param.15) | copy-start | bytes 3145732
  7.2 161.0 %all-reduce.2.cloned.1.call-start = ((), (), s32[]{:S(2)}) async-start(), calls=%async_computation.1 | async-start | bytes 2097152 | tf_op jit(solution)/shard_map/psum | solution.py:46
  14.0 2.5 copy-start.8
  14.0 2.5 copy-start.9
  16.4 284.9 %reduce-scatter.4.cloned.1.call-start = ((), (), s32[]{:S(2)}) async-start(), calls=%async_computation.2 | async-start | bytes 5013504
  22.7 5.9 %copy-start.7 = (f32[2048]{0:T(1024)S(1)}, f32[2048]{0:T(1024)}, u32[]{:S(2)}) copy-start(f32[2048]{0:T(1024)} %param.13) | copy-start | bytes 24580
  28.6 5.4 %copy-start.3 = (bf16[2048,3,256]{0,2,1:T(8,128)(2,1)S(1)}, bf16[2048,3,256]{0,2,1:T(8,128)(2,1)}, u32[]{:S(2)}) copy-start(bf16[2048,3,256]{0,2,1:T(8,128)(2,1)} %copy.62) | copy-start | bytes 9437188
  32.1 1.9 copy-start.2
  170.8 0.7 copy-start.5
  172.6 14.6 %copy-start.6 = (bf16[4,12288]{1,0:T(4,128)(2,1)S(1)}, bf16[4,12288]{1,0:T(4,128)(2,1)}, u32[]{:S(2)}) copy-start(bf16[4,12288]{1,0:T(4,128)(2,1)} %get-tuple-element.13) | copy-start | bytes 294916
  174.1 1.6 collective-permute-start
  175.7 7.4 %collective-permute-start.1 = (f32[1024,48]{0,1:T(8,128)S(1)}, f32[1024,48]{0,1:T(8,128)S(1)}, u32[]{:S(2)}, u32[]{:S(2)}) collective-permute-start(f32[1024,48]{0,1:T(8,128)S(1)} %add.162), channel_id=1, source_target_pairs={{0,2},{1,3},{2,0},{3,1},{4,6},{5,7},{6,4},{7,5},{8,10},{9,11},{10,... | collective-permute-start | bytes 589832 | tf_op jit(solution)/shard_map/ppermute | solution.py:27
  183.1 8.2 %collective-permute-start.2 = (f32[1024,48]{0,1:T(8,128)S(1)}, f32[1024,48]{0,1:T(8,128)S(1)}, u32[]{:S(2)}, u32[]{:S(2)}) collective-permute-start(f32[1024,48]{0,1:T(8,128)S(1)} %add.163), channel_id=1, source_target_pairs={{0,4},{1,5},{2,6},{3,7},{4,0},{5,1},{6,2},{7,3},{8,12},{9,13},{10,... | collective-permute-start | bytes 589832 | tf_op jit(solution)/shard_map/ppermute | solution.py:27
  193.8 1.8 copy-start.1
  197.1 38.1 %collective-permute-start.3 = (bf16[1024,256]{0,1:T(8,128)(2,1)}, bf16[1024,256]{0,1:T(8,128)(2,1)}, u32[]{:S(2)}, u32[]{:S(2)}) collective-permute-start(bf16[1024,256]{0,1:T(8,128)(2,1)} %bitcast.106), channel_id=1, source_target_pairs={{0,8},{8,16},{16,24},{24,32},{32,40},{40,48},{48,56},{56,64},{64,7... | collective-permute-start | bytes 1572872 | tf_op jit(solution)/shard_map/ppermute | solution.py:16
  204.8 18.3 %collective-permute-start.4 = (bf16[1024,256]{0,1:T(8,128)(2,1)}, bf16[1024,256]{0,1:T(8,128)(2,1)}, u32[]{:S(2)}, u32[]{:S(2)}) collective-permute-start(bf16[1024,256]{0,1:T(8,128)(2,1)} %bitcast.29), channel_id=1, source_target_pairs={{0,8},{8,16},{16,24},{24,32},{32,40},{40,48},{48,56},{56,64},{64,7... | collective-permute-start | bytes 1572872 | tf_op jit(solution)/shard_map/ppermute | solution.py:16
  258.8 0.7 copy-start.10
  258.8 1.3 copy-start.4
Sparse Core Ops, SparseCore 0:
  16.6 151.6 all-reduce.1
  259.0 42.3 reduce-scatter.3
where the time goes:
time: 314 us; the launch traced here: 312 us
  waiting for transfers between devices  183 us (58%)
  local copies, waits for them, and re-layouts  40.9 us (13%)
  matrix products  34.3 us (11%)
  other arithmetic  26.4 us (8%)
  between operations  15.9 us (5%)
  starting transfers between devices  12.3 us (4%)
    psum x1, waiting for transfers between devices, fetch_adapters(): compact = lax.psum(compact, 'grp')  129 us
    unnamed x3, waiting for transfers between devices  36.7 us
    unnamed x34, local copies, waits for them, and re-layouts  15.3 us
    sub x1, matrix products, local(): weights = jnp.exp(scores - row_top)  10.8 us
    ppermute x2, waiting for transfers between devices, shifted(): return lax.ppermute(block, axis, route)  10.3 us
    dot_general x1, matrix products, local(): jnp.einsum('hts,shd->thd', weights_bf, value_all, preferred_element_type=...  8.93 us
    ppermute x2, starting transfers between devices, shifted(): return lax.ppermute(block, axis, route)  7.3 us
    ppermute x3, waiting for transfers between devices, xor_allreduce(): value = value + lax.ppermute(value, axis, route)  6.53 us
  transfers between devices with their start and end apart: 7, of which 5 were waited for; matrix products, arithmetic and copies ran while one was open for 16% of the time, Pallas kernels for 0%

commit v1 on v0

--- a/solution.py
+++ b/solution.py
@@ -43,7 +43,7 @@
     local_idx = slots % held
     flat = jnp.concatenate([s.reshape(held, -1) for s in stores], axis=1)
     compact = jnp.where(mine[:, None], jnp.take(flat, local_idx, axis=0), jnp.zeros((), flat.dtype))
-    compact = lax.psum(compact, "grp")
+    compact = jnp.sum(lax.all_gather(compact, "grp"), axis=0)
     mine_rows = jnp.take(compact, rank[wanted], axis=0)
     out = []
     at = 0

time: 314 us -> 400 us (1.27)
  waiting for transfers between devices: 183 us -> 262 us
  other arithmetic: 26.4 us -> 34 us
    all_gather x0 -> x1, waiting for transfers between devices: none -> 213 us  [fetch_adapters(): compact = jnp.sum(lax.all_gather(compact, 'grp'), axis=0)]
    psum x1 -> x0, waiting for transfers between devices: 129 us -> none  [fetch_adapters(): compact = lax.psum(compact, 'grp')]
    reduce_sum x0 -> x1, other arithmetic: none -> 11.4 us  [fetch_adapters(): compact = jnp.sum(lax.all_gather(compact, 'grp'), axis=0)]
    ppermute x2, waiting for transfers between devices: 10.3 us -> 4.58 us  [shifted(): return lax.ppermute(block, axis, route)]
    unnamed x34 -> x42, local copies, waits for them, and re-layouts: 15.3 us -> 16.6 us
  transfers between devices with their start and end apart: 7 -> 7, of which waited for: 5 -> 5; matrix products, arithmetic and copies ran while one was open for 16% -> 12% of each run, Pallas kernels for 0% -> 0%
where the time goes in v1:
time: 400 us; the launch traced here: 399 us
  waiting for transfers between devices  262 us (66%)
  local copies, waits for them, and re-layouts  41.7 us (10%)
  matrix products  34.3 us (9%)
  other arithmetic  34 us (8%)
  between operations  15.9 us (4%)
  starting transfers between devices  11.3 us (3%)
    all_gather x1, waiting for transfers between devices, fetch_adapters(): compact = jnp.sum(lax.all_gather(compact, 'grp'), axis=0)  213 us
    unnamed x3, waiting for transfers between devices  36.5 us
    unnamed x42, local copies, waits for them, and re-layouts  16.6 us
    reduce_sum x1, other arithmetic, fetch_adapters(): compact = jnp.sum(lax.all_gather(compact, 'grp'), axis=0)  11.4 us
    sub x1, matrix products, local(): weights = jnp.exp(scores - row_top)  10.8 us
    dot_general x1, matrix products, local(): jnp.einsum('hts,shd->thd', weights_bf, value_all, preferred_element_type=...  8.93 us
  transfers between devices with their start and end apart: 7, of which 5 were waited for; matrix products, arithmetic and copies ran while one was open for 12% of the time, Pallas kernels for 0%

profile of v1, /device:TPU:4, one launch (start us, length us, event | category | flops | bytes accessed | tf_op | source)
XLA Modules:
  0.0 398.9 jit_solution(16586959923026743653)
XLA Ops:
  7.2 0.8 copy.93
  8.0 0.8 copy.66
  9.0 0.8 copy.92
  9.9 0.9 copy.65
  11.0 0.8 copy.63
  12.5 1.3 gather_fusion.1
  14.0 1.2 gather_fusion.2
  15.2 1.2 fusion.20
  19.4 4.7 %copy.62 = bf16[2048,3,256]{0,2,1:T(8,128)(2,1)} copy(bf16[2048,3,256]{2,0,1:T(8,128)(2,1)} %param.14) | data formatting | bytes 6291456 | tf_op args[2]
  24.4 3.2 fusion.2
  28.2 1.6 fusion.11
  29.8 1.0 fusion.4
  30.8 2.0 copy-done.3
  32.9 5.1 %fusion.9 = f32[1024,3,256]{0,2,1:T(8,128)} fusion(bf16[1024,2048]{1,0:T(8,128)(2,1)S(1)} %fusion.4, bf16[2048,3,256]{0,2,1:T(8,128)(2,1)S(1)} %copy-done.6), kind=kOutput, calls=%fused_computation.21 | convolution fusion | flops 3221225472 | bytes 10485760 | tf_op jit(solution)/shard_map/dot_general | solution.py:131
  38.0 212.9 %all-gather.2.cloned.1.call-done = bf16[32,16,32768]{2,1,0:T(8,128)(2,1)} async-done(((bf16[1,16,32768]{2,1,0:T(8,128)(2,1)}), bf16[32,16,32768]{2,1,0:T(8,128)(2,1)}) %all-gather.2.cloned.1.call-update) | async-done | bytes 33554448 | tf_op jit(solution)/shard_map/all_gather | solution.py:46
  250.9 11.4 %reduce_sum.91 = bf16[16,32768]{1,0:T(8,128)(2,1)S(1)} reduce(bf16[32,16,32768]{2,1,0:T(8,128)(2,1)} %all-gather.2.cloned.1.call-done, bf16[]{:T(256)} %constant.124.clone.1), dimensions={0}, to_apply=%region_4.5 | reduce | flops 16252928 | bytes 34603008 | tf_op jit(solution)/shard_map/reduce_sum | solution.py:46
  262.2 0.8 gather_fusion.3
  265.0 1.4 fusion.22
  266.6 1.5 pad_add_fusion
  268.2 1.8 collective-permute-start.1
  269.9 1.9 multiply_cosine_fusion
  271.8 3.9 collective-permute-done.1
  275.8 3.1 collective-permute-start.2
  278.9 0.8 fusion.48
  280.0 3.7 collective-permute-done.2
  283.8 2.5 bitcast_add_fusion
  286.3 1.5 fusion.47
  288.6 0.9 slice.89
  289.4 1.5 copy.89
  291.7 1.0 copy.71
  292.7 2.8 collective-permute-start.4
  295.5 1.6 copy.88
  297.1 3.5 collective-permute-start.3
  300.6 2.1 slice_bitcast_fusion
  302.7 2.5 subtract_convert_fusion
  305.2 4.6 %collective-permute-done.4 = bf16[1024,256]{0,1:T(8,128)(2,1)} collective-permute-done((bf16[1024,256]{0,1:T(8,128)(2,1)}, bf16[1024,256]{0,1:T(8,128)(2,1)}, u32[]{:S(2)}, u32[]{:S(2)}) %collective-permute-start.4) | collective-permute-done | bytes 524320 | tf_op jit(solution)/shard_map/ppermute | solution.py:16
  309.7 1.3 copy.72
  311.1 10.8 %fusion.50 = (f32[2,1024]{1,0:T(2,128)S(1)}, f32[2,1024,2048]{2,1,0:T(8,128)}) fusion(pred[1024,2048]{1,0:T(8,128)(4,1)} %pad_add_fusion, bf16[1024,2,128]{2,0,1:T(8,128)(2,1)S(1)} %maximum_convert_fusion, bf16[1024,2,128]{2,0,1:T(8,128)(2,1)S(1)} %copy.72, bf16[1024,2,64]{2,0,1:T(8,128)(2,1)} %get-tuple-element.7, bf16[1024,2,64]{2,0,1:T(8,128)(2,1)} %get-tuple-element.6), kind=kOutput, calls=%fused_computation.128 | convolution fusion | flops 1093666816 | bytes 20455424 | tf_op jit(solution)/shard_map/sub | solution.py:159
  321.9 8.9 %fusion.16 = bf16[2,128,1024]{2,1,0:T(8,128)(2,1)S(1)} fusion(f32[2,1024,2048]{2,1,0:T(8,128)} %get-tuple-element.23, f32[2,1024]{1,0:T(2,128)S(1)} %get-tuple-element.22, bf16[1024,2,128]{0,2,1:T(8,128)(2,1)S(1)} %copy-done.9, bf16[1024,2,128]{0,2,1:T(8,128)(2,1)} %bitcast.23), kind=kOutput, calls=%fused_computation.32 | convolution fusion | flops 1084489728 | bytes 18358272 | tf_op jit(solution)/shard_map/hts,shd->thd/dot_general | solution.py:161
  331.1 3.2 convolution_convert_fusion
  334.3 6.4 %copy.82 = bf16[1024,2048]{0,1:T(8,128)(2,1)} copy(bf16[1024,2048]{1,0:T(8,128)(2,1)} %convolution_convert_fusion) | data formatting | bytes 8388608 | tf_op jit(solution)/shard_map/reshape | solution.py:171
  340.8 4.7 %pad_maximum_fusion = bf16[1024,8,272]{0,2,1:T(8,128)(2,1)} fusion(bf16[1024,8,16]{0,2,1:T(8,128)(2,1)S(1)} %broadcast_in_dim.158, bf16[1024,8,256]{0,2,1:T(8,128)(2,1)} %bitcast.101), kind=kLoop, calls=%fused_computation.20 | loop fusion | flops 8912896 | bytes 8912896 | tf_op jit(solution)/shard_map/concatenate | solution.py:169
  347.3 1.1 reshape.520
  348.4 1.1 pad_maximum_fusion.2
  350.2 1.1 broadcast_select_fusion
  351.3 36.5 %reduce-scatter.4.cloned.1.call-done = bf16[272,1024]{1,0:T(8,128)(2,1)} async-done(((bf16[2176,1024]{1,0:T(8,128)(2,1)}), bf16[272,1024]{1,0:T(8,128)(2,1)}) %reduce-scatter.4.cloned.1.call-update) | async-done | bytes 557072
  388.6 1.1 slice.77
  389.9 2.2 fusion.15
  (99 shorter events, 11.3 us)
Async XLA Ops:
  7.2 323.9 %copy-start = (bf16[256,2048]{1,0:T(8,128)(2,1)S(1)}, bf16[256,2048]{1,0:T(8,128)(2,1)}, u32[]{:S(2)}) copy-start(bf16[256,2048]{1,0:T(8,128)(2,1)} %param.15) | copy-start | bytes 3145732
  7.2 243.7 %all-gather.2.cloned.1.call-start = ((), (), s32[]{:S(2)}) async-start(), calls=%async_computation.1 | async-start | bytes 34603008 | tf_op jit(solution)/shard_map/all_gather | solution.py:46
  14.0 2.5 copy-start.12
  14.0 2.5 copy-start.13
  16.4 371.4 %reduce-scatter.4.cloned.1.call-start = ((), (), s32[]{:S(2)}) async-start(), calls=%async_computation.2 | async-start | bytes 5013504
  24.2 5.6 %copy-start.11 = (f32[2048]{0:T(1024)S(1)}, f32[2048]{0:T(1024)}, u32[]{:S(2)}) copy-start(f32[2048]{0:T(1024)} %param.13) | copy-start | bytes 24580
  24.2 5.6 %copy-start.1 = (bf16[1024,2048]{1,0:T(8,128)(2,1)S(1)}, bf16[1024,2048]{1,0:T(8,128)(2,1)}, u32[]{:S(2)}) copy-start(bf16[1024,2048]{1,0:T(8,128)(2,1)} %param.12) | copy-start | bytes 12582916
  29.8 3.1 copy-start.6
  30.8 2.0 copy-start.3
  263.1 3.6 copy-start.5
  263.2 0.7 copy-start.8
  266.4 13.6 %copy-start.10 = (bf16[4,12288]{1,0:T(4,128)(2,1)S(1)}, bf16[4,12288]{1,0:T(4,128)(2,1)}, u32[]{:S(2)}) copy-start(bf16[4,12288]{1,0:T(4,128)(2,1)} %get-tuple-element.13) | copy-start | bytes 294916
  266.5 1.7 collective-permute-start
  268.2 7.5 %collective-permute-start.1 = (f32[1024,48]{0,1:T(8,128)S(1)}, f32[1024,48]{0,1:T(8,128)S(1)}, u32[]{:S(2)}, u32[]{:S(2)}) collective-permute-start(f32[1024,48]{0,1:T(8,128)S(1)} %add.160), channel_id=1, source_target_pairs={{0,2},{1,3},{2,0},{3,1},{4,6},{5,7},{6,4},{7,5},{8,10},{9,11},{10,... | collective-permute-start | bytes 589832 | tf_op jit(solution)/shard_map/ppermute | solution.py:27
  271.8 19.2 %copy-start.4 = (f32[1024,64]{1,0:T(8,128)}, f32[1024,64]{1,0:T(8,128)S(1)}, u32[]{:S(2)}) copy-start(f32[1024,64]{1,0:T(8,128)S(1)} %get-tuple-element.15) | copy-start | bytes 786436
  275.8 8.0 %collective-permute-start.2 = (f32[1024,48]{0,1:T(8,128)S(1)}, f32[1024,48]{0,1:T(8,128)S(1)}, u32[]{:S(2)}, u32[]{:S(2)}) collective-permute-start(f32[1024,48]{0,1:T(8,128)S(1)} %add.161), channel_id=1, source_target_pairs={{0,4},{1,5},{2,6},{3,7},{4,0},{5,1},{6,2},{7,3},{8,12},{9,13},{10,... | collective-permute-start | bytes 589832 | tf_op jit(solution)/shard_map/ppermute | solution.py:27
  286.3 2.3 copy-start.2
  292.7 17.0 %collective-permute-start.4 = (bf16[1024,256]{0,1:T(8,128)(2,1)}, bf16[1024,256]{0,1:T(8,128)(2,1)}, u32[]{:S(2)}, u32[]{:S(2)}) collective-permute-start(bf16[1024,256]{0,1:T(8,128)(2,1)} %bitcast.30), channel_id=1, source_target_pairs={{0,8},{8,16},{16,24},{24,32},{32,40},{40,48},{48,56},{56,64},{64,7... | collective-permute-start | bytes 1572872 | tf_op jit(solution)/shard_map/ppermute | solution.py:16
  297.1 24.8 %collective-permute-start.3 = (bf16[1024,256]{0,1:T(8,128)(2,1)}, bf16[1024,256]{0,1:T(8,128)(2,1)}, u32[]{:S(2)}, u32[]{:S(2)}) collective-permute-start(bf16[1024,256]{0,1:T(8,128)(2,1)} %bitcast.110), channel_id=1, source_target_pairs={{0,8},{8,16},{16,24},{24,32},{32,40},{40,48},{48,56},{56,64},{64,7... | collective-permute-start | bytes 1572872 | tf_op jit(solution)/shard_map/ppermute | solution.py:16
  311.1 10.8 %copy-start.9 = (bf16[1024,2,128]{0,2,1:T(8,128)(2,1)S(1)}, bf16[1024,2,128]{0,2,1:T(8,128)(2,1)}, u32[]{:S(2)}) copy-start(bf16[1024,2,128]{0,2,1:T(8,128)(2,1)} %slice_bitcast_fusion) | copy-start | bytes 1572868
  345.5 0.7 copy-start.14
  345.5 1.3 copy-start.7
Sparse Core Ops, SparseCore 0:
  16.5 234.2 all-gather.1
  345.6 42.1 reduce-scatter.3
